TPU v7x, 512 devices: a whole 4x4x16 slice. The times are simulated.
512 devices in a mesh: dp: 16 (over z_hi, x), seq: 32 (over y, z_lo, core).
Axes of the slice: x: 4, y: 4, z: 16 (z_hi: 4, z_lo: 4; z = z_hi * 4 + z_lo), core: 2. Of those that a mesh axis runs over, the one named last changes fastest.
Arguments:
- binned_signals: bfloat16 [16, 16384, 768], P('dp', 'seq'), may hold values from -6 to 6
- kernel_coefficients: bfloat16 [5, 768, 768], P(None, 'dp'), may hold values from -0.09375 to 0.09375
- asking_projector: bfloat16 [768, 256], replicated, may hold values from -0.21875 to 0.21875
- lookup_projector: bfloat16 [768, 256], replicated, may hold values from -0.21875 to 0.21875
- content_projector: bfloat16 [768, 384], replicated, may hold values from -0.21875 to 0.21875
- readout_projector: bfloat16 [384, 768], replicated, may hold values from -0.3125 to 0.3125
- logit_multipliers: float32 [4], replicated, may hold values from 8 to 24
- loss_sensitivity: bfloat16 [16, 4096, 768], P('dp', 'seq'), may hold values from -0.0234375 to 0.0234375
Outputs:
- pooled: bfloat16 [16, 4096, 768], P('dp', 'seq')
- update: float32 [16, 4096, 768], P('dp', 'seq')
- query_grad: float32 [768, 256], replicated
- out_grad: float32 [384, 768], replicated
All inputs are finite; a program needn't handle non-finite values.
Results may differ from a plain program's by a relative error of at most 0.0095.
The roundings to bfloat16 on the way count: a program that leaves them out, or rounds other values in their place, can miss the bound.
Values may be sent and summed in bfloat16 or wider, within the bound.
No kernel may reach another device: no remote copies, remote signals or barrier semaphores. Data moves between devices by JAX's collectives and lax.ppermute only.
A program may use at most 128 MiB of HBM per device.

v0:
```python
import jax
import jax.numpy as jnp
from jax import lax
from jax.sharding import PartitionSpec as P

POOL = 4
norm_eps = 1e-05
head_eps = 1e-06


def padded_2(array, sides, width):
    for axis, dim in sides:
        devices, length = (lax.axis_size(axis), array.shape[dim])
        up = [(i, (i + 1) % devices) for i in range(devices - 1)]
        down = [(j, i) for i, j in up]
        last = lax.slice_in_dim(array, length - width, length, axis=dim)
        leading = lax.slice_in_dim(array, 0, width, axis=dim)
        before = lax.ppermute(last, axis, up)
        after = lax.ppermute(leading, axis, down)
        array = jnp.concatenate([before, array, after], axis=dim)
    return array


def layer_norm(values):
    centre = jnp.mean(values, axis=-1, keepdims=True)
    shifted = values - centre
    variance = jnp.mean(shifted * shifted, axis=-1, keepdims=True)
    return shifted * lax.rsqrt(variance + norm_eps)


def activate(values):
    return values * jax.nn.sigmoid(1.702 * values)


def head_norm(values, group_width):
    grouped = values.reshape(values.shape[0], -1, group_width)
    factor = lax.rsqrt(jnp.mean(grouped * grouped, axis=-1, keepdims=True) + head_eps)
    return (
        (grouped * factor).reshape(values.shape),
        jnp.broadcast_to(factor, grouped.shape).reshape(values.shape),
    )


def contract_first(former, latter):
    return lax.dot_general(
        former, latter, (((0,), (0,)), ((), ())), preferred_element_type=jnp.float32
    )


def contract_last(former, latter):
    return lax.dot_general(
        former, latter, (((1,), (1,)), ((), ())), preferred_element_type=jnp.float32
    )


def stacked_conv(padded, all_taps, length_fine):
    tap_count = all_taps.shape[0]
    windows = jnp.concatenate(
        [padded[tap_index : tap_index + length_fine] for tap_index in range(tap_count)], axis=1
    )
    flat_taps = all_taps.reshape(tap_count * all_taps.shape[1], all_taps.shape[2])
    return jnp.dot(windows, flat_taps, preferred_element_type=jnp.float32)


def on_device(
    binned_signals,
    kernel_coefficients,
    asking_projector,
    lookup_projector,
    content_projector,
    readout_projector,
    logit_multipliers,
    loss_sensitivity,
):
    incoming_tensor = binned_signals[0]
    directional_perturbations = loss_sensitivity[0]
    length_fine = incoming_tensor.shape[0]
    channels = incoming_tensor.shape[1]
    tap_count = kernel_coefficients.shape[0]
    margin = tap_count // 2
    attender_total = logit_multipliers.shape[0]
    probe_extent = asking_projector.shape[1] // attender_total
    value_width = content_projector.shape[1] // attender_total
    activated = activate(layer_norm(incoming_tensor.astype(jnp.float32))).astype(jnp.bfloat16)
    padded = padded_2(activated, (("seq", 0),), margin)
    all_taps = lax.all_gather(kernel_coefficients, "dp", axis=1, tiled=True)
    conv_sum = stacked_conv(padded, all_taps, length_fine)
    summed = incoming_tensor.astype(jnp.float32) + conv_sum
    pooled = jnp.max(summed.reshape(length_fine // POOL, POOL, channels), axis=1).astype(
        jnp.bfloat16
    )
    normed = layer_norm(pooled.astype(jnp.float32)).astype(jnp.bfloat16)
    queries = jnp.dot(normed, asking_projector, preferred_element_type=jnp.float32)
    query_hat, query_factor = head_norm(queries, probe_extent)
    query_unit = query_hat.astype(jnp.bfloat16)
    key_local = head_norm(
        jnp.dot(normed, lookup_projector, preferred_element_type=jnp.float32), probe_extent
    )[0].astype(jnp.bfloat16)
    value_local = jnp.dot(normed, content_projector, preferred_element_type=jnp.float32).astype(
        jnp.bfloat16
    )
    key_unit, values_all = (
        lax.all_gather(key_local, "seq", axis=0, tiled=True),
        lax.all_gather(value_local, "seq", axis=0, tiled=True),
    )
    heads_grad = contract_last(directional_perturbations, readout_projector).astype(jnp.bfloat16)
    outputs = []
    diffs = []
    for attender_slot in range(attender_total):
        key_lo = attender_slot * probe_extent
        value_lo = attender_slot * value_width
        query_part = query_unit[:, key_lo : key_lo + probe_extent]
        key_part = key_unit[:, key_lo : key_lo + probe_extent]
        value_part = values_all[:, value_lo : value_lo + value_width]
        attender_logit_gain = logit_multipliers[attender_slot] / probe_extent
        scores = contract_last(query_part, key_part) * attender_logit_gain
        expo = jnp.exp(scores)
        probs = expo / jnp.sum(expo, axis=1, keepdims=True)
        head_out = jnp.dot(
            probs.astype(jnp.bfloat16), value_part, preferred_element_type=jnp.float32
        )
        outputs.append(head_out)
        grad_part = heads_grad[:, value_lo : value_lo + value_width]
        prob_grad = contract_last(grad_part, value_part)
        delta = jnp.sum(grad_part.astype(jnp.float32) * head_out, axis=1, keepdims=True)
        score_grad = (probs * (prob_grad - delta)).astype(jnp.bfloat16)
        unit_grad = (
            jnp.dot(score_grad, key_part, preferred_element_type=jnp.float32) * attender_logit_gain
        )
        hat_part = query_hat[:, key_lo : key_lo + probe_extent]
        factor_part = query_factor[:, key_lo : key_lo + probe_extent]
        diffs.append(
            factor_part
            * (unit_grad - hat_part * jnp.mean(hat_part * unit_grad, axis=1, keepdims=True))
        )
    heads_low = jnp.concatenate(outputs, axis=1).astype(jnp.bfloat16)
    update = jnp.dot(heads_low, readout_projector, preferred_element_type=jnp.float32)
    query_diff = jnp.concatenate(diffs, axis=1).astype(jnp.bfloat16)
    query_local = contract_first(normed, query_diff)
    out_local = contract_first(heads_low, directional_perturbations)
    query_grad, out_grad = lax.psum((query_local, out_local), ("dp", "seq"))
    return (pooled[None], update[None], query_grad, out_grad)


def solution(mesh):
    return jax.shard_map(
        on_device,
        mesh=mesh,
        in_specs=(
            P("dp", "seq", None),
            P(None, "dp", None),
            P(),
            P(),
            P(),
            P(),
            P(),
            P("dp", "seq", None),
        ),
        out_specs=(P("dp", "seq", None), P("dp", "seq", None), P(), P()),
        check_vma=False,
    )
```

profile of v0, /device:TPU:2, one launch (start us, length us, event | category | flops | bytes accessed | tf_op | source)
XLA Modules:
  0.0 843.0 jit_solution(14659338999122518173)
XLA Ops:
  7.2 0.7 all-gather.4.cloned.1.call-update
  8.0 1.3 convert_reduce_fusion
  9.3 1.5 fusion.23
  10.8 0.6 fusion.22
  11.4 1.7 collective-permute-start
  13.2 1.3 collective-permute-start.1
  14.5 1.1 fusion.67
  15.6 1.1 fusion.69
  16.7 1.5 constant_dynamic-update-slice_fusion
  18.3 1.1 fusion.65
  19.4 1.2 fusion.68
  20.6 163.3 %all-gather.4.cloned.1.call-done = bf16[5,768,768]{2,1,0:T(8,128)(2,1)} async-done(((bf16[5,48,768]{2,1,0:T(8,128)(2,1)}), bf16[5,768,768]{2,1,0:T(8,128)(2,1)}) %all-gather.4.cloned.1.call-update) | async-done | bytes 5898256 | tf_op jit(solution)/shard_map/all_gather | solution.py:86
  183.9 7.1 fusion.12
  191.2 1.0 reduce_max.9
  192.4 0.2 fusion.72
  192.7 0.3 fusion.113
  193.2 0.6 multiply_convert_fusion
  193.9 1.0 convolution_convert_fusion.1
  194.9 0.2 all-reduce.3.cloned.1.call-start
  195.1 0.7 fusion.112
  198.4 0.3 convolution_convert_fusion
  198.7 0.3 fusion.114
  199.3 55.0 %all-gather.6.cloned.1.call-done = bf16[4096,256]{1,0:T(8,128)(2,1)} async-done(((bf16[128,256]{1,0:T(8,128)(2,1)}), bf16[4096,256]{1,0:T(8,128)(2,1)}) %all-gather.6.cloned.1.call-update) | async-done | bytes 2097168 | tf_op jit(solution)/shard_map/all_gather | solution.py:103
  254.3 3.3 fusion.118
  257.5 1.8 fusion.117
  259.4 1.9 fusion.116
  261.3 2.3 fusion.115
  263.7 58.5 %all-gather.8.cloned.1.call-done = bf16[4096,384]{1,0:T(8,128)(2,1)} async-done(((bf16[128,384]{1,0:T(8,128)(2,1)}), bf16[4096,384]{1,0:T(8,128)(2,1)}) %all-gather.8.cloned.1.call-update) | async-done | bytes 3145744 | tf_op jit(solution)/shard_map/all_gather | solution.py:104
  322.1 3.0 fusion.36
  325.2 0.4 copy-done.23
  325.6 1.0 fusion.38
  326.7 0.5 copy-done.5
  327.2 1.0 fusion.40
  328.2 0.5 copy-done.4
  328.8 1.1 multiply_reduce_fusion.7
  329.9 3.7 fusion.31
  333.7 3.9 fusion.30
  337.6 4.1 fusion.29
  341.6 4.0 multiply_reduce_fusion.3
  345.6 0.7 broadcast_multiply_fusion.3
  346.3 0.6 broadcast_multiply_fusion.1
  346.9 1.1 fusion.80
  348.1 1.3 fusion.81
  349.4 1.3 fusion.74
  350.7 1.0 convolution_bitcast_fusion
  351.7 481.5 %all-reduce.3.cloned.1.call-done = (f32[768,256]{1,0:T(8,128)}, f32[384,768]{1,0:T(8,128)}) async-done(((f32[768,256]{1,0:T(8,128)}, f32[384,768]{1,0:T(8,128)}), (f32[768,256]{1,0:T(8,128)}, f32[384,768]{1,0:T(8,128)})) %all-reduce.3.cloned.1.call-update) | async-done | bytes 1966096 | tf_op jit(solution)/shard_map/psum | solution.py:141
  833.3 2.2 copy.41
  835.4 1.0 copy.42
  (75 shorter events, 1.1 us)
Async XLA Ops:
  7.2 191.2 %copy-start = (bf16[384,768]{1,0:T(8,128)(2,1)S(1)}, bf16[384,768]{1,0:T(8,128)(2,1)}, u32[]{:S(2)}) copy-start(bf16[384,768]{1,0:T(8,128)(2,1)} %param.13) | copy-start | bytes 1769476
  7.2 3.6 copy-start.1
  7.2 176.7 %all-gather.4.cloned.1.call-start = ((), (), s32[]{:S(2)}) async-start(), calls=%async_computation | async-start | bytes 6266880 | tf_op jit(solution)/shard_map/all_gather | solution.py:86
  7.9 246.3 %all-gather.6.cloned.1.call-start = ((), (), s32[]{:S(2)}) async-start(), calls=%async_computation.1 | async-start | bytes 2162688 | tf_op jit(solution)/shard_map/all_gather | solution.py:103
  11.4 3.0 collective-permute-start
  13.2 5.1 collective-permute-start.1
  191.0 1.7 copy-start.9
  191.2 2.7 copy-start.24
  191.2 3.9 copy-start.13
  191.2 7.1 copy-start.8
  192.3 155.8 %copy-start.3 = (bf16[128,768]{1,0:T(8,128)(2,1)}, bf16[128,768]{1,0:T(8,128)(2,1)S(1)}, u32[]{:S(2)}) copy-start(bf16[128,768]{1,0:T(8,128)(2,1)S(1)} %reduce_max.9) | copy-start | bytes 589828
  192.4 6.3 copy-start.10
  192.4 6.5 copy-start.11
  192.6 6.3 copy-start.14
  193.9 128.3 %all-gather.8.cloned.1.call-start = ((), (), s32[]{:S(2)}) async-start(), calls=%async_computation.2 | async-start | bytes 3244032 | tf_op jit(solution)/shard_map/all_gather | solution.py:104
  194.9 638.4 %all-reduce.3.cloned.1.call-start = ((), (), s32[]{:S(2)}) async-start(), calls=%async_computation.3 | async-start | bytes 3932160 | tf_op jit(solution)/shard_map/psum | solution.py:141
  254.3 3.3 copy-start.2
  257.5 64.6 %copy-start.21 = (f32[128]{0:T(128)}, f32[128]{0:T(128)S(1)}, u32[]{:S(2)}) copy-start(f32[128]{0:T(128)S(1)} %get-tuple-element.40) | copy-start | bytes 1540
  259.4 65.8 %copy-start.19 = (f32[128]{0:T(128)}, f32[128]{0:T(128)S(1)}, u32[]{:S(2)}) copy-start(f32[128]{0:T(128)S(1)} %get-tuple-element.38) | copy-start | bytes 1540
  261.3 65.3 %copy-start.17 = (f32[128]{0:T(128)}, f32[128]{0:T(128)S(1)}, u32[]{:S(2)}) copy-start(f32[128]{0:T(128)S(1)} %get-tuple-element.36) | copy-start | bytes 1540
  322.1 3.0 copy-start.6
  322.1 3.5 copy-start.23
  325.6 1.6 copy-start.5
  327.2 1.6 copy-start.4
  327.2 1.6 copy-start.16
  328.8 1.1 copy-start.22
  329.9 3.7 copy-start.20
  333.7 3.9 copy-start.18
  333.7 3.9 copy-start.25
  341.6 6.5 copy-start.12
  341.6 6.5 copy-start.15
  833.3 2.2 copy-start.7
Sparse Core Ops, SparseCore 0:
  11.0 172.8 all-gather.3
  194.0 60.2 all-gather.5
  257.0 65.0 all-gather.7
  350.8 482.3 all-reduce.2
where the time goes:
time: 843 us
  waiting for transfers between devices  759 us (90%)
  matrix products  43.8 us (5%)
  between operations  16.7 us (2%)
  other arithmetic  14 us (2%)
    psum x1, waiting for transfers between devices, on_device(): query_grad, out_grad = lax.psum((query_local, out_local), ('dp', 'seq'))  482 us
    all_gather x1, waiting for transfers between devices, on_device(): all_taps = lax.all_gather(kernel_coefficients, 'dp', axis=1, tiled=True)  163 us
    all_gather x1, waiting for transfers between devices, on_device(): lax.all_gather(value_local, 'seq', axis=0, tiled=True)  58.5 us
    all_gather x1, waiting for transfers between devices, on_device(): lax.all_gather(key_local, 'seq', axis=0, tiled=True)  55 us
  transfers between devices with their start and end apart: 6, of which 4 were waited for; matrix products, arithmetic and copies ran while one was open for 3% of the time, Pallas kernels for 0%

commit v1 on v0

--- a/solution.py
+++ b/solution.py
@@ -101,7 +101,9 @@
     )
     key_unit, values_all = (
         lax.all_gather(key_local, "seq", axis=0, tiled=True),
-        lax.all_gather(value_local, "seq", axis=0, tiled=True),
+        jnp.concatenate(
+            lax.all_to_all(jnp.stack([value_local] * lax.axis_size("seq")), "seq", 0, 0), axis=0
+        ),
     )
     heads_grad = contract_last(directional_perturbations, readout_projector).astype(jnp.bfloat16)
     outputs = []

time: 843 us -> 815 us (0.967)
  waiting for transfers between devices: 759 us -> 721 us
    all_gather x1 -> x0, waiting for transfers between devices: 58.5 us -> none  [on_device(): lax.all_gather(value_local, 'seq', axis=0, tiled=True)]
    all_gather x1, waiting for transfers between devices: 55 us -> 77.9 us  [on_device(): lax.all_gather(key_local, 'seq', axis=0, tiled=True)]
  transfers between devices with their start and end apart: 6 -> 6, of which waited for: 4 -> 3; matrix products, arithmetic and copies ran while one was open for 3% -> 3% of each run, Pallas kernels for 0% -> 0%
where the time goes in v1:
time: 815 us
  waiting for transfers between devices  721 us (88%)
  matrix products  47.9 us (6%)
  between operations  16.7 us (2%)
  other arithmetic  14.1 us (2%)
  starting transfers between devices  8.27 us (1%)
    psum x1, waiting for transfers between devices, on_device(): query_grad, out_grad = lax.psum((query_local, out_local), ('dp', 'seq'))  479 us
    all_gather x1, waiting for transfers between devices, on_device(): all_taps = lax.all_gather(kernel_coefficients, 'dp', axis=1, tiled=True)  163 us
    all_gather x1, waiting for transfers between devices, on_device(): lax.all_gather(key_local, 'seq', axis=0, tiled=True)  77.9 us
  transfers between devices with their start and end apart: 6, of which 3 were waited for; matrix products, arithmetic and copies ran while one was open for 3% of the time, Pallas kernels for 0%

profile of v1, /device:TPU:2, one launch (start us, length us, event | category | flops | bytes accessed | tf_op | source)
XLA Modules:
  0.0 814.7 jit_solution(17917103347367748334)
XLA Ops:
  7.2 0.7 all-gather.3.cloned.1.call-update
  7.9 1.3 convert_reduce_fusion
  9.2 1.5 fusion.23
  10.8 0.6 fusion.22
  11.4 1.7 collective-permute-start
  13.1 1.3 collective-permute-start.1
  14.4 1.1 fusion.67
  15.6 1.1 fusion.69
  16.7 1.5 constant_dynamic-update-slice_fusion
  18.2 1.1 fusion.65
  19.3 1.2 fusion.68
  20.5 163.4 %all-gather.3.cloned.1.call-done = bf16[5,768,768]{2,1,0:T(8,128)(2,1)} async-done(((bf16[5,48,768]{2,1,0:T(8,128)(2,1)}), bf16[5,768,768]{2,1,0:T(8,128)(2,1)}) %all-gather.3.cloned.1.call-update) | async-done | bytes 5898256 | tf_op jit(solution)/shard_map/all_gather | solution.py:86
  183.9 7.1 fusion.12
  191.0 0.2 reshape.110
  191.2 1.0 reduce_max.9
  192.2 0.1 convert_reduce_fusion.1
  192.4 0.2 fusion.72
  192.6 0.3 convolution_convert_fusion.1
  192.9 2.2 stack.2
  195.1 4.9 all-to-all-start
  200.1 0.3 fusion.113
  200.7 0.6 multiply_convert_fusion
  201.3 0.2 all-reduce.3.cloned.1.call-start
  201.6 0.6 fusion.112
  204.7 0.3 convolution_convert_fusion
  205.0 0.3 fusion.114
  205.6 77.9 %all-gather.5.cloned.1.call-done = bf16[4096,256]{1,0:T(8,128)(2,1)} async-done(((bf16[128,256]{1,0:T(8,128)(2,1)}), bf16[4096,256]{1,0:T(8,128)(2,1)}) %all-gather.5.cloned.1.call-update) | async-done | bytes 2097168 | tf_op jit(solution)/shard_map/all_gather | solution.py:103
  283.5 3.3 fusion.116
  286.9 1.7 fusion.117
  288.6 1.9 fusion.118
  290.6 2.3 fusion.115
  292.9 3.4 fusion.40
  296.3 2.8 fusion.38
  299.1 2.4 fusion.36
  301.6 2.4 multiply_reduce_fusion.7
  304.0 3.8 fusion.31
  307.8 3.9 fusion.30
  311.6 4.1 fusion.29
  315.7 4.0 multiply_reduce_fusion.3
  319.7 0.7 broadcast_multiply_fusion.3
  320.4 0.7 broadcast_multiply_fusion.1
  321.1 1.1 fusion.80
  322.2 1.3 fusion.81
  323.5 1.3 fusion.74
  324.8 1.0 convolution_bitcast_fusion
  325.9 479.1 %all-reduce.3.cloned.1.call-done = (f32[768,256]{1,0:T(8,128)}, f32[384,768]{1,0:T(8,128)}) async-done(((f32[768,256]{1,0:T(8,128)}, f32[384,768]{1,0:T(8,128)}), (f32[768,256]{1,0:T(8,128)}, f32[384,768]{1,0:T(8,128)})) %all-reduce.3.cloned.1.call-update) | async-done | bytes 1966096 | tf_op jit(solution)/shard_map/psum | solution.py:143
  805.0 2.2 copy.41
  807.1 1.0 copy.42
  (73 shorter events, 0.7 us)
Async XLA Ops:
  7.2 197.5 %copy-start = (bf16[384,768]{1,0:T(8,128)(2,1)S(1)}, bf16[384,768]{1,0:T(8,128)(2,1)}, u32[]{:S(2)}) copy-start(bf16[384,768]{1,0:T(8,128)(2,1)} %param.13) | copy-start | bytes 1769476
  7.2 3.6 copy-start.1
  7.2 176.7 %all-gather.3.cloned.1.call-start = ((), (), s32[]{:S(2)}) async-start(), calls=%async_computation.1 | async-start | bytes 6266880 | tf_op jit(solution)/shard_map/all_gather | solution.py:86
  11.4 3.0 collective-permute-start
  13.1 5.1 collective-permute-start.1
  191.0 1.6 copy-start.23
  192.2 130.0 %copy-start.3 = (bf16[128,768]{1,0:T(8,128)(2,1)}, bf16[128,768]{1,0:T(8,128)(2,1)S(1)}, u32[]{:S(2)}) copy-start(bf16[128,768]{1,0:T(8,128)(2,1)S(1)} %reduce_max.9) | copy-start | bytes 589828
  192.4 12.6 %copy-start.11 = (f32[128]{0:T(128)}, f32[128]{0:T(128)S(1)}, u32[]{:S(2)}) copy-start(f32[128]{0:T(128)S(1)} %broadcast_multiply_fusion.5) | copy-start | bytes 1540
  192.6 12.4 %copy-start.14 = (f32[128]{0:T(128)}, f32[128]{0:T(128)S(1)}, u32[]{:S(2)}) copy-start(f32[128]{0:T(128)S(1)} %add_rsqrt_fusion.3) | copy-start | bytes 1540
  195.1 5.0 copy-start.9
  195.1 6.5 copy-start.13
  195.1 97.8 %all-to-all-start = ((bf16[32,128,384]{2,1,0:T(8,128)(2,1)}), bf16[32,128,384]{2,1,0:T(8,128)(2,1)}, u32[]{:S(2)}, u32[]{:S(2)}) async-start(bf16[32,128,384]{2,1,0:T(8,128)(2,1)} %stack.2), calls=%async_computation | async-start | bytes 6291456 | tf_op jit(solution)/shard_map/all_to_all | solution.py:105
  200.1 4.6 copy-start.8
  200.1 5.0 copy-start.10
  200.1 83.4 %all-gather.5.cloned.1.call-start = ((), (), s32[]{:S(2)}) async-start(), calls=%async_computation.2 | async-start | bytes 2162688 | tf_op jit(solution)/shard_map/all_gather | solution.py:103
  201.3 603.6 %all-reduce.3.cloned.1.call-start = ((), (), s32[]{:S(2)}) async-start(), calls=%async_computation.3 | async-start | bytes 3932160 | tf_op jit(solution)/shard_map/psum | solution.py:143
  283.5 3.4 copy-start.2
  286.9 6.0 copy-start.17
  288.6 7.7 copy-start.19
  290.6 8.5 %copy-start.21 = (f32[128]{0:T(128)}, f32[128]{0:T(128)S(1)}, u32[]{:S(2)}) copy-start(f32[128]{0:T(128)S(1)} %get-tuple-element.40) | copy-start | bytes 1540
  292.9 3.4 copy-start.5
  296.3 2.8 copy-start.6
  299.1 2.4 copy-start.4
  299.1 2.4 copy-start.16
  301.6 2.4 copy-start.22
  304.0 3.8 copy-start.20
  307.7 3.9 copy-start.18
  307.8 3.9 copy-start.24
  315.7 6.5 copy-start.12
  315.7 6.5 copy-start.15
  805.0 2.2 copy-start.7
Sparse Core Ops, SparseCore 0:
  11.0 172.8 all-gather.2
  203.6 79.8 all-gather.4
  325.0 479.9 all-reduce.2
